TPU v7x, 256 devices: a whole 4x4x8 slice. The times are simulated.
256 devices in a mesh: req: 32 (over x, y, core), kv: 8 (over z).
Axes of the slice: x: 4, y: 4, z: 8, core: 2. Of those that a mesh axis runs over, the one named last changes fastest.
Arguments:
- hidden: bfloat16 [512, 1536], P('req'), may hold values from -6 to 6
- norm_gain: float32 [1536], replicated, may hold values from 0.5 to 1.5
- w_qkv: bfloat16 [1536, 3072], P(None, 'kv'), may hold values from -0.15625 to 0.15625
- w_out: bfloat16 [1536, 1536], P(None, 'kv'), may hold values from -0.15625 to 0.15625
- cache_pages: bfloat16 [6144, 2, 8, 96, 128], P('req', None, 'kv'), may hold values from -340 to 340
- lengths: int32 [512], P('req'), may hold values from 1 to 16384, as said below
- page_table: int32 [512, 128], P('req'), may hold values from 0 to 191, as said below
- occupant: int32 [512], replicated, may hold values from 0 to 511, each once
Outputs:
- mixed: bfloat16 [512, 1536], P('req', 'kv')
Inputs may be any that keep to these rules, and one draw needn't show every extreme that they name: `occupant`: every request is served at exactly one slot. Slot s holds ceil(lengths[s] / 128) pages; on every index of req the pages of its 16 slots fit its pool of 192, some pool is full, and some request has 16384 tokens. `page_table`: the first ceil(lengths[s] / 128) entries of slot s are pages of its own pool that no other slot of that pool uses; later entries are arbitrary pages of the pool.
All inputs are finite; a program needn't handle non-finite values.
Results may differ from a plain program's by a relative error of at most 0.0043.
Values may be sent and summed in bfloat16 or wider, within the bound.
No kernel may reach another device: no remote copies, remote signals or barrier semaphores. Data moves between devices by JAX's collectives and lax.ppermute only.
A program may use at most 64 MiB of HBM per device.

v0:
```python
import math
import jax
import jax.numpy as jnp
from jax import lax
from jax.sharding import PartitionSpec as P

HD = 96
PAGE = 128
MAXP = 128
GROUP = 2


def per_device(hidden, norm_gain, w_qkv, w_out, cache_pages, lengths, page_table, occupant):
    slot_count = hidden.shape[0]
    pool_size = cache_pages.shape[0]
    kv_local = cache_pages.shape[2]
    first_slot = lax.axis_index("req") * slot_count
    hidden_wide = hidden.astype(jnp.float32)
    normed = (
        hidden_wide
        * lax.rsqrt(jnp.mean(hidden_wide * hidden_wide, axis=1, keepdims=True) + 1e-05)
        * norm_gain
    ).astype(jnp.bfloat16)
    served = lax.dynamic_slice_in_dim(occupant, first_slot, slot_count)
    every_normed = lax.all_gather(normed, "req", axis=0, tiled=True)
    picked = jnp.take(every_normed, served, axis=0)
    slot_rows = jnp.dot(picked, w_qkv, preferred_element_type=jnp.float32).astype(jnp.bfloat16)
    slot_rows = slot_rows.reshape(slot_count, kv_local, GROUP + 2, HD)
    queries = slot_rows[:, :, :GROUP]
    own_key = slot_rows[:, :, GROUP]
    own_value = slot_rows[:, :, GROUP + 1]
    score_scale = 1.0 / math.sqrt(HD)
    pages_used = (lengths + PAGE - 1) // PAGE
    live_page = jnp.arange(MAXP, dtype=jnp.int32)[None, :] < pages_used[:, None]
    matches = (
        (page_table[:, :, None] == jnp.arange(pool_size, dtype=jnp.int32)[None, None, :])
        & live_page[:, :, None]
    ).astype(jnp.int32)
    owner_table = jnp.sum(matches, axis=1)
    slot_ids = jnp.arange(slot_count, dtype=jnp.int32)
    page_owner = jnp.sum(owner_table * slot_ids[:, None], axis=0)
    page_rank = jnp.sum(matches * jnp.arange(MAXP, dtype=jnp.int32)[None, :, None], axis=(0, 1))
    page_limit = jnp.sum(owner_table * lengths[:, None], axis=0)
    offsets = page_rank[:, None] * PAGE + jnp.arange(PAGE, dtype=jnp.int32)[None, :]
    token_live = offsets < page_limit[:, None]
    page_queries = jnp.take(queries, page_owner, axis=0)
    scores = (
        jnp.einsum(
            "pgjd,pgdt->pgjt", page_queries, cache_pages[:, 0], preferred_element_type=jnp.float32
        )
        * score_scale
    )
    scores = jnp.where(token_live[:, None, None, :], scores, -jnp.inf)
    page_max = jnp.max(scores, axis=-1)
    own_score = (
        jnp.sum(queries.astype(jnp.float32) * own_key.astype(jnp.float32)[:, :, None, :], axis=-1)
        * score_scale
    )
    owner_mask = owner_table > 0
    slot_max = jnp.max(jnp.where(owner_mask[:, :, None, None], page_max[None], -jnp.inf), axis=1)
    slot_max = jnp.maximum(slot_max, own_score)
    weights = jnp.exp(scores - jnp.take(slot_max, page_owner, axis=0)[..., None])
    rounded = weights.astype(jnp.bfloat16)
    page_total = jnp.sum(weights, axis=-1)
    page_numerator = jnp.einsum(
        "pgjt,pgdt->pgjd", rounded, cache_pages[:, 1], preferred_element_type=jnp.float32
    )
    own_weight = jnp.exp(own_score - slot_max)
    own_rounded = lax.optimization_barrier(own_weight.astype(jnp.bfloat16)).astype(jnp.float32)
    owner_float = owner_table.astype(jnp.float32)
    denominator = (
        jnp.einsum("sp,pgj->sgj", owner_float, page_total, precision=lax.Precision.HIGHEST)
        + own_weight
    )
    numerator = jnp.einsum(
        "sp,pgjd->sgjd", owner_float, page_numerator, precision=lax.Precision.HIGHEST
    )
    numerator = numerator + own_rounded[..., None] * own_value.astype(jnp.float32)[:, :, None, :]
    context = (numerator / denominator[..., None]).astype(jnp.bfloat16).reshape(slot_count, -1)
    gathered = lax.all_gather(context, "req", axis=0, tiled=True)
    wanted = first_slot + slot_ids
    selector = (occupant[None, :] == wanted[:, None]).astype(jnp.bfloat16)
    attended = jnp.dot(selector, gathered, preferred_element_type=jnp.float32).astype(jnp.bfloat16)
    partial_value = lax.dot_general(
        attended, w_out, (((1,), (1,)), ((), ())), preferred_element_type=jnp.float32
    )
    summed = lax.psum_scatter(partial_value, "kv", scatter_dimension=1, tiled=True)
    col_share = summed.shape[1]
    residual = lax.dynamic_slice_in_dim(hidden_wide, lax.axis_index("kv") * col_share, col_share, 1)
    return (residual + summed).astype(jnp.bfloat16)


def solution(mesh):
    return jax.shard_map(
        per_device,
        mesh=mesh,
        in_specs=(
            P("req", None),
            P(),
            P(None, "kv"),
            P(None, "kv"),
            P("req", None, "kv", None, None),
            P("req"),
            P("req", None),
            P(),
        ),
        out_specs=P("req", "kv"),
        check_vma=False,
    )
```

profile of v0, /device:TPU:2, one launch (start us, length us, event | category | flops | bytes accessed | tf_op | source)
XLA Modules:
  0.0 147.1 jit_solution(2917014156746804395)
XLA Ops:
  6.5 1.0 multiply_reduce_fusion
  7.6 1.5 %multiply_convert_fusion = bf16[16,1536]{1,0:T(8,128)(2,1)} fusion(f32[1536]{0:T(1024)} %param.9, f32[16]{0:T(128)S(1)} %add_rsqrt_fusion, bf16[16,1536]{1,0:T(8,128)(2,1)} %param.8), kind=kLoop, calls=%fused_computation.28 | loop fusion | flops 98304 | bytes 104512 | tf_op jit(solution)/shard_map/convert_element_type | solution.py:23
  9.1 0.0 reduce-scatter.4.cloned.1.call-start
  9.2 0.8 compare_and_fusion
  10.0 0.7 and_select_fusion
  10.6 0.1 iota_compare_fusion.1
  10.7 1.7 %select_reduce_fusion = (s32[192]{0:T(256)S(1)}, s32[16,192]{1,0:T(8,128)S(1)}) fusion(s32[16,128]{1,0:T(8,128)} %param.14, pred[16,128]{1,0:T(8,128)(4,1)S(1)} %iota_compare_fusion.1), kind=kLoop, calls=%fused_computation.10 | loop fusion | flops 2356032 | bytes 23296 | tf_op jit(solution)/shard_map/reduce_sum | solution.py:42
  12.4 0.7 multiply_reduce_fusion.2
  13.2 0.1 add_compare_fusion
  13.3 47.2 %all-gather.2.cloned.1.call-done = bf16[512,1536]{1,0:T(8,128)(2,1)} async-done(((bf16[16,1536]{1,0:T(8,128)(2,1)}), bf16[512,1536]{1,0:T(8,128)(2,1)}) %all-gather.2.cloned.1.call-update) | async-done | bytes 1572880 | tf_op jit(solution)/shard_map/all_gather | solution.py:25
  60.5 2.2 %gather_fusion = bf16[16,1536]{1,0:T(8,128)(2,1)S(1)} fusion(bf16[512,1536]{1,0:T(8,128)(2,1)} %all-gather.2.cloned.1.call-done, s32[1024]{0:T(1024)S(1)} %pad_clamp_fusion.1), kind=kCustom, calls=%fused_computation | custom fusion | bytes 98368 | tf_op jit(solution)/shard_map/jit(_take)/gather | solution.py:26
  62.7 0.3 convolution_convert_fusion
  63.1 0.1 reshape.230
  63.2 0.1 multiply_reduce_fusion.1
  63.3 0.1 copy.28
  63.4 0.8 gather_fusion.1
  64.2 3.8 %fusion.39 = (f32[192,2]{1,0:T(8,128)S(1)}, f32[192,2,128]{2,1,0:T(2,128)S(1)}) fusion(bf16[192,2,1,96,128]{4,3,2,1,0:T(8,128)(2,1)} %param.12, bf16[192,2,96]{2,1,0:T(2,128)(2,1)S(1)} %gather_fusion.1, pred[192]{0:T(512)(128)(4,1)S(1)} %compare_and_fusion.1, pred[192,128]{1,0:T(8,128)(4,1)S(1)} %add_compare_fusion), kind=kOutput, calls=%fused_computation.76 | convolution fusion | flops 9621120 | bytes 5015232 | tf_op jit(solution)/shard_map/pgjd,pgdt->pgjt/dot_general | solution.py:48
  68.1 0.1 copy.27
  68.2 0.1 select_reduce_fusion.1
  68.3 0.1 copy.29
  68.4 0.7 gather_fusion.2
  69.1 0.1 broadcast_select_fusion.2
  69.2 5.0 %fusion = f32[192,2,96]{2,1,0:T(2,128)S(1)} fusion(bf16[192,2,1,96,128]{4,3,2,1,0:T(8,128)(2,1)} %param.12, f32[192,2,128]{2,1,0:T(2,128)S(1)} %get-tuple-element.16, f32[192,2]{1,0:T(8,128)S(1)} %broadcast_select_fusion.2), kind=kOutput, calls=%fused_computation.3 | convolution fusion | flops 9535488 | bytes 5064192 | tf_op jit(solution)/shard_map/pgjt,pgdt->pgjd/dot_general | solution.py:65
  74.2 0.5 fusion.16
  74.8 0.3 convolution_add_fusion.1
  75.0 0.3 fusion.11
  75.3 0.1 reshape.233
  75.4 23.2 %all_gather.7 = bf16[512,192]{1,0:T(8,128)(2,1)S(1)} all-gather(bf16[16,192]{1,0:T(8,128)(2,1)S(1)} %reshape.233), channel_id=1, replica_groups=mesh['req'=32,'kv'=8] {'req'}, dimensions={0}, use_global_device_ids=true | all-gather | bytes 202752 | tf_op jit(solution)/shard_map/all_gather | solution.py:80
  98.6 1.5 %convolution_bitcast_fusion = f32[1536,16]{1,0:T(8,128)} fusion(bf16[1536,192]{0,1:T(8,128)(2,1)S(1)} %copy-done.1, bf16[512,192]{1,0:T(8,128)(2,1)S(1)} %all_gather.7, s32[512]{0:T(512)S(1)} %copy-done.3, s32[16]{0:T(128)S(1)} %iota_add_fusion), kind=kOutput, calls=%fused_computation.9 | convolution fusion | flops 12594176 | bytes 886848
  100.2 38.5 %reduce-scatter.4.cloned.1.call-done = f32[192,16]{1,0:T(8,128)} async-done(((f32[1536,16]{1,0:T(8,128)}), f32[192,16]{1,0:T(8,128)}) %reduce-scatter.4.cloned.1.call-update) | async-done | bytes 12304
  138.6 0.9 copy.34
  139.6 0.7 add_convert_fusion
  (25 shorter events, 0.2 us)
Async XLA Ops:
  6.5 56.2 %copy-start = (bf16[1536,384]{1,0:T(8,128)(2,1)S(1)}, bf16[1536,384]{1,0:T(8,128)(2,1)}, u32[]{:S(2)}) copy-start(bf16[1536,384]{1,0:T(8,128)(2,1)} %param.10) | copy-start | bytes 3538948
  6.5 53.9 %all-gather.2.cloned.1.call-start = ((), (), s32[]{:S(2)}) async-start(), calls=%async_computation.1 | async-start | bytes 1622016 | tf_op jit(solution)/shard_map/all_gather | solution.py:25
  9.1 129.5 %reduce-scatter.4.cloned.1.call-start = ((), (), s32[]{:S(2)}) async-start(), calls=%async_computation.2 | async-start | bytes 884736
  69.2 29.5 %copy-start.1 = (bf16[1536,192]{0,1:T(8,128)(2,1)S(1)}, bf16[1536,192]{0,1:T(8,128)(2,1)}, u32[]{:S(2)}) copy-start(bf16[1536,192]{0,1:T(8,128)(2,1)} %param.11) | copy-start | bytes 1769476
  69.2 29.4 %copy-start.3 = (s32[512]{0:T(512)S(1)}, s32[512]{0:T(512)}, u32[]{:S(2)}) copy-start(s32[512]{0:T(512)} %param.15) | copy-start | bytes 6148
  74.7 25.4 %copy-start.2 = (bf16[16,1536]{1,0:T(8,128)(2,1)S(1)}, bf16[16,1536]{1,0:T(8,128)(2,1)}, u32[]{:S(2)}) copy-start(bf16[16,1536]{1,0:T(8,128)(2,1)} %param.8) | copy-start | bytes 147460
Sparse Core Ops, SparseCore 0:
  9.9 50.5 all-gather.1
  100.2 38.3 reduce-scatter.3
where the time goes:
time: 147 us
  waiting for transfers between devices  85.7 us (58%)
  blocking collectives  23.2 us (16%)
  between operations  13.6 us (9%)
  matrix products  11.2 us (8%)
  other arithmetic  8.17 us (6%)
  local copies, waits for them, and re-layouts  5.21 us (4%)
    all_gather x1, waiting for transfers between devices, per_device(): every_normed = lax.all_gather(normed, 'req', axis=0, tiled=True)  47.2 us
    unnamed x3, waiting for transfers between devices  38.5 us
    all_gather x1, blocking collectives, per_device(): gathered = lax.all_gather(context, 'req', axis=0, tiled=True)  23.2 us
    dot_general x1, matrix products, per_device(): jnp.einsum('pgjt,pgdt->pgjd', rounded, cache_pages[:, 1], preferred_eleme...  5.01 us
    dot_general x1, matrix products, per_device(): jnp.einsum('pgjd,pgdt->pgjt', page_queries, cache_pages[:, 0], preferred_...  3.85 us
  transfers between devices with their start and end apart: 2, of which 2 were waited for; matrix products, arithmetic and copies ran while one was open for 3% of the time, Pallas kernels for 0%

commit v1 on v0

--- a/solution.py
+++ b/solution.py
@@ -22,7 +22,15 @@
         * norm_gain
     ).astype(jnp.bfloat16)
     served = lax.dynamic_slice_in_dim(occupant, first_slot, slot_count)
-    every_normed = lax.all_gather(normed, "req", axis=0, tiled=True)
+    every_normed = jnp.concatenate(
+        lax.all_to_all(
+            jnp.stack([normed] * lax.axis_size("req"), 0),
+            axis_name="req",
+            split_axis=0,
+            concat_axis=0,
+        ),
+        0,
+    )
     picked = jnp.take(every_normed, served, axis=0)
     slot_rows = jnp.dot(picked, w_qkv, preferred_element_type=jnp.float32).astype(jnp.bfloat16)
     slot_rows = slot_rows.reshape(slot_count, kv_local, GROUP + 2, HD)

time: 147 us -> 125 us (0.85)
  waiting for transfers between devices: 85.7 us -> 57.9 us
  starting transfers between devices: 0.04 us -> 7.8 us
  other arithmetic: 8.17 us -> 4.88 us
  blocking collectives: 23.2 us -> 24.9 us
    all_gather x1 -> x0, waiting for transfers between devices: 47.2 us -> none  [per_device(): every_normed = lax.all_gather(normed, 'req', axis=0, tiled=True)]
    all_to_all x0 -> x1, waiting for transfers between devices: none -> 18.6 us  [per_device(): lax.all_to_all(jnp.stack([normed] * lax.axis_size('req'), 0), axis_name='...]
    all_to_all x0 -> x1, starting transfers between devices: none -> 7.75 us  [per_device(): lax.all_to_all(jnp.stack([normed] * lax.axis_size('req'), 0), axis_name='...]
    gather x1, local copies, waits for them, and re-layouts: 2.25 us -> 0.59 us  [per_device(): picked = jnp.take(every_normed, served, axis=0)]
    all_gather x1, blocking collectives: 23.2 us -> 24.9 us  [per_device(): gathered = lax.all_gather(context, 'req', axis=0, tiled=True)]
    unnamed x3 -> x2, waiting for transfers between devices: 38.5 us -> 39.3 us
  transfers between devices with their start and end apart: 2 -> 2, of which waited for: 2 -> 2; matrix products, arithmetic and copies ran while one was open for 3% -> 1% of each run, Pallas kernels for 0% -> 0%
where the time goes in v1:
time: 125 us
  waiting for transfers between devices  57.9 us (46%)
  blocking collectives  24.9 us (20%)
  between operations  13.6 us (11%)
  matrix products  11.2 us (9%)
  starting transfers between devices  7.8 us (6%)
  local copies, waits for them, and re-layouts  4.89 us (4%)
  other arithmetic  4.88 us (4%)
    unnamed x2, waiting for transfers between devices  39.3 us
    all_gather x1, blocking collectives, per_device(): gathered = lax.all_gather(context, 'req', axis=0, tiled=True)  24.9 us
    all_to_all x1, waiting for transfers between devices, per_device(): lax.all_to_all(jnp.stack([normed] * lax.axis_size('req'), 0), axis_name='...  18.6 us
    all_to_all x1, starting transfers between devices, per_device(): lax.all_to_all(jnp.stack([normed] * lax.axis_size('req'), 0), axis_name='...  7.75 us
    dot_general x1, matrix products, per_device(): jnp.einsum('pgjt,pgdt->pgjd', rounded, cache_pages[:, 1], preferred_eleme...  5.01 us
    dot_general x1, matrix products, per_device(): jnp.einsum('pgjd,pgdt->pgjt', page_queries, cache_pages[:, 0], preferred_...  3.84 us
  transfers between devices with their start and end apart: 2, of which 2 were waited for; matrix products, arithmetic and copies ran while one was open for 1% of the time, Pallas kernels for 0%

profile of v1, /device:TPU:2, one launch (start us, length us, event | category | flops | bytes accessed | tf_op | source)
XLA Modules:
  0.0 125.1 jit_solution(12680022186596960200)
XLA Ops:
  6.5 1.0 multiply_reduce_fusion
  7.6 0.9 multiply_convert_fusion
  8.5 1.3 %stack.2 = bf16[32,16,1536]{2,1,0:T(8,128)(2,1)} broadcast(bf16[16,1536]{1,0:T(8,128)(2,1)S(1)} %multiply_convert_fusion), dimensions={1,2} | broadcast | bytes 1622016 | tf_op jit(solution)/shard_map/stack | solution.py:27
  9.8 7.8 %all-to-all-start = ((bf16[32,16,1536]{2,1,0:T(8,128)(2,1)}), bf16[32,16,1536]{2,1,0:T(8,128)(2,1)S(1)}, u32[]{:S(2)}, u32[]{:S(2)}) async-start(bf16[32,16,1536]{2,1,0:T(8,128)(2,1)} %stack.2), calls=%async_computation | async-start | bytes 3145728 | tf_op jit(solution)/shard_map/all_to_all | solution.py:26
  17.6 0.1 compare_and_fusion
  17.8 0.1 iota_compare_fusion.1
  17.8 1.0 select_reduce_fusion
  18.8 0.1 multiply_reduce_fusion.2
  19.0 0.1 add_compare_fusion
  19.1 18.6 %all-to-all-done = bf16[32,16,1536]{2,1,0:T(8,128)(2,1)S(1)} async-done(((bf16[32,16,1536]{2,1,0:T(8,128)(2,1)}), bf16[32,16,1536]{2,1,0:T(8,128)(2,1)S(1)}, u32[]{:S(2)}, u32[]{:S(2)}) %all-to-all-start) | async-done | bytes 1572896 | tf_op jit(solution)/shard_map/all_to_all | solution.py:26
  37.7 0.6 gather_fusion
  38.3 0.3 convolution_convert_fusion
  38.6 0.1 reshape.236
  38.8 0.1 multiply_reduce_fusion.1
  38.9 0.1 copy.28
  38.9 0.8 gather_fusion.1
  39.8 3.8 %fusion.39 = (f32[192,2]{1,0:T(8,128)S(1)}, f32[192,2,128]{2,1,0:T(2,128)S(1)}) fusion(bf16[192,2,1,96,128]{4,3,2,1,0:T(8,128)(2,1)} %param.12, bf16[192,2,96]{2,1,0:T(2,128)(2,1)S(1)} %gather_fusion.1, pred[192]{0:T(512)(128)(4,1)S(1)} %compare_and_fusion.1, pred[192,128]{1,0:T(8,128)(4,1)S(1)} %add_compare_fusion), kind=kOutput, calls=%fused_computation.76 | convolution fusion | flops 9621120 | bytes 5015232 | tf_op jit(solution)/shard_map/pgjd,pgdt->pgjt/dot_general | solution.py:56
  43.6 0.1 copy.27
  43.7 0.1 select_reduce_fusion.1
  43.8 0.1 copy.29
  43.9 0.7 gather_fusion.2
  44.6 0.1 broadcast_select_fusion.2
  44.7 5.0 %fusion = f32[192,2,96]{2,1,0:T(2,128)S(1)} fusion(bf16[192,2,1,96,128]{4,3,2,1,0:T(8,128)(2,1)} %param.12, f32[192,2,128]{2,1,0:T(2,128)S(1)} %get-tuple-element.16, f32[192,2]{1,0:T(8,128)S(1)} %broadcast_select_fusion.2), kind=kOutput, calls=%fused_computation.3 | convolution fusion | flops 9535488 | bytes 5064192 | tf_op jit(solution)/shard_map/pgjt,pgdt->pgjd/dot_general | solution.py:73
  49.7 0.5 fusion.16
  50.3 0.3 convolution_add_fusion.1
  50.5 0.3 fusion.11
  50.8 0.1 reshape.239
  50.9 24.9 %all_gather.3 = bf16[512,192]{1,0:T(8,128)(2,1)S(1)} all-gather(bf16[16,192]{1,0:T(8,128)(2,1)S(1)} %reshape.239), channel_id=1, replica_groups=mesh['req'=32,'kv'=8] {'req'}, dimensions={0}, use_global_device_ids=true | all-gather | bytes 202752 | tf_op jit(solution)/shard_map/all_gather | solution.py:88
  75.8 1.5 %convolution_bitcast_fusion = f32[1536,16]{1,0:T(8,128)} fusion(bf16[1536,192]{0,1:T(8,128)(2,1)S(1)} %copy-done.1, bf16[512,192]{1,0:T(8,128)(2,1)S(1)} %all_gather.3, s32[512]{0:T(512)S(1)} %copy-done.4, s32[16]{0:T(128)S(1)} %iota_add_fusion), kind=kOutput, calls=%fused_computation.9 | convolution fusion | flops 12594176 | bytes 886848
  77.3 39.3 %reduce-scatter.4.cloned.1.call-done = f32[192,16]{1,0:T(8,128)} async-done(((f32[1536,16]{1,0:T(8,128)}), f32[192,16]{1,0:T(8,128)}) %reduce-scatter.4.cloned.1.call-update) | async-done | bytes 12304
  116.7 0.9 copy.34
  117.6 0.7 add_convert_fusion
  (29 shorter events, 0.2 us)
Async XLA Ops:
  6.5 31.8 %copy-start = (bf16[1536,384]{1,0:T(8,128)(2,1)S(1)}, bf16[1536,384]{1,0:T(8,128)(2,1)}, u32[]{:S(2)}) copy-start(bf16[1536,384]{1,0:T(8,128)(2,1)} %param.10) | copy-start | bytes 3538948
  9.8 7.8 %copy-start.4 = (s32[512]{0:T(512)S(1)}, s32[512]{0:T(512)}, u32[]{:S(2)}) copy-start(s32[512]{0:T(512)} %param.15) | copy-start | bytes 6148
  9.8 7.9 %copy-start.5 = (s32[16]{0:T(128)S(1)}, s32[16]{0:T(128)}, u32[]{:S(2)}) copy-start(s32[16]{0:T(128)} %param.13) | copy-start | bytes 196
  9.8 8.0 %copy-start.3 = (s32[16,128]{1,0:T(8,128)S(1)}, s32[16,128]{1,0:T(8,128)}, u32[]{:S(2)}) copy-start(s32[16,128]{1,0:T(8,128)} %param.14) | copy-start | bytes 24580
  9.8 27.9 %all-to-all-start = ((bf16[32,16,1536]{2,1,0:T(8,128)(2,1)}), bf16[32,16,1536]{2,1,0:T(8,128)(2,1)S(1)}, u32[]{:S(2)}, u32[]{:S(2)}) async-start(bf16[32,16,1536]{2,1,0:T(8,128)(2,1)} %stack.2), calls=%async_computation | async-start | bytes 3145728 | tf_op jit(solution)/shard_map/all_to_all | solution.py:26
  17.6 99.1 %reduce-scatter.4.cloned.1.call-start = ((), (), s32[]{:S(2)}) async-start(), calls=%async_computation.2 | async-start | bytes 884736
  44.7 31.1 %copy-start.1 = (bf16[1536,192]{0,1:T(8,128)(2,1)S(1)}, bf16[1536,192]{0,1:T(8,128)(2,1)}, u32[]{:S(2)}) copy-start(bf16[1536,192]{0,1:T(8,128)(2,1)} %param.11) | copy-start | bytes 1769476
  50.3 27.0 %copy-start.2 = (bf16[16,1536]{1,0:T(8,128)(2,1)S(1)}, bf16[16,1536]{1,0:T(8,128)(2,1)}, u32[]{:S(2)}) copy-start(bf16[16,1536]{1,0:T(8,128)(2,1)} %param.8) | copy-start | bytes 147460
Sparse Core Ops, SparseCore 0:
  77.4 39.1 reduce-scatter.3
